TPU v7x, 512 devices: a whole 4x8x8 slice. The times are simulated.
512 devices in a mesh: section: 32 (over z, x), neuron: 16 (over y, core).
Axes of the slice: x: 4, y: 8, z: 8, core: 2. Of those that a mesh axis runs over, the one named last changes fastest.
Arguments:
- inputs: bfloat16 [6, 32768], P(None, 'neuron'), may hold values from 0 to 2
- weight_tiles: bfloat16 [32, 2048, 128, 128], P('section', 'neuron'), may hold values from -0.07324219 to 0.07910156
- source_block: int32 [32, 2048], P('section', 'neuron'), may hold values from 0 to 255
- target_block: int32 [32, 2048], P('section', 'neuron'), may hold values from 0 to 15
- live_slots: int32 [32, 16], P('section', 'neuron'), may hold values from 16 to 128, as said below
Outputs:
- activations: bfloat16 [32, 6, 32768], P('section', None, 'neuron')
Inputs may be any that keep to these rules, and one draw needn't show every extreme that they name: live_slots[l, n] is 128, 64, 32 or 16, and in every layer some shard has all 128 slots live.
All inputs are finite; a program needn't handle non-finite values.
Results may differ from a plain program's by a relative error of at most 0.0045.
Values may be sent and summed in bfloat16 or wider, within the bound.
No kernel may reach another device: no remote copies, remote signals or barrier semaphores. Data moves between devices by JAX's collectives and lax.ppermute only.
A program may use at most 64 MiB of HBM per device.

v0:
```python
import jax
import jax.numpy as jnp
from jax import lax
from jax.sharding import PartitionSpec as P

NEURON_BIAS = -0.3
CLIP_LEVEL = 32.0
UNROLL = True


def layer_apply(gathered, weight_tiles, source, selector):
    row_count = gathered.shape[0]
    block_size = weight_tiles.shape[2]
    column_count = selector.shape[1]
    block_count = gathered.shape[1] // block_size
    shaped = gathered.reshape(row_count, block_count, block_size)
    picked = shaped.at[:, source].get(mode="promise_in_bounds")
    partial_value = jnp.einsum(
        "msk,skj->msj", picked, weight_tiles[0], preferred_element_type=jnp.float32
    )
    summed = jnp.einsum("msj,sc->mcj", partial_value, selector, precision=lax.Precision.HIGHEST)
    result = jnp.clip(summed + NEURON_BIAS, 0.0, CLIP_LEVEL).astype(jnp.bfloat16)
    return result.reshape(row_count, column_count * block_size)


def local(inputs, weight_tiles, source_block, target_block, live_slots):
    section_pos = lax.axis_index("section")
    section_count = lax.axis_size("section")
    row_count, shard_width = inputs.shape
    slot_count = weight_tiles.shape[1]
    column_count = shard_width // weight_tiles.shape[2]
    source = source_block[0]
    live_mask = jnp.arange(slot_count, dtype=jnp.int32) < live_slots[0, 0]
    selector = (
        (target_block[0][:, None] == jnp.arange(column_count, dtype=jnp.int32)[None, :])
        & live_mask[:, None]
    ).astype(jnp.float32)

    def compute(gathered):
        return layer_apply(gathered, weight_tiles, source, selector)

    def empty(gathered):
        return jnp.zeros((row_count, shard_width), jnp.bfloat16)

    def step(step_num, current, collected, route):
        gathered = lax.all_gather(current, "neuron", axis=1, tiled=True)
        active = section_pos == step_num
        result = compute(gathered)
        collected = jnp.where(active, result, collected)
        if route is None:
            return (result, collected)
        return (lax.ppermute(result, "section", route), collected)

    collected = jnp.zeros((row_count, shard_width), jnp.bfloat16)
    current = inputs
    if UNROLL:
        for t in range(section_count - 1):
            current, collected = step(t, current, collected, [(t, t + 1)])
    else:
        route = [(i, i + 1) for i in range(section_count - 1)]
        current, collected = lax.fori_loop(
            0, section_count - 1, lambda t, c: step(t, c[0], c[1], route), (current, collected)
        )
    _, collected = step(section_count - 1, current, collected, None)
    return collected[None]


def solution(mesh):
    in_specs = (
        P(None, "neuron"),
        P("section", "neuron", None, None),
        P("section", "neuron"),
        P("section", "neuron"),
        P("section", "neuron"),
    )
    out_specs = P("section", None, "neuron")
    return jax.shard_map(local, mesh=mesh, in_specs=in_specs, out_specs=out_specs, check_vma=False)
```

profile of v0, /device:TPU:455, one launch (start us, length us, event | category | flops | bytes accessed | tf_op | source)
XLA Modules:
  0.0 809.9 jit_solution(16794483580277421957)
XLA Ops:
  0.7 19.8 %all_gather.96 = bf16[6,32768]{1,0:T(8,128)(2,1)S(1)} all-gather(bf16[6,2048]{1,0:T(8,128)(2,1)} %param.5), channel_id=1, replica_groups=mesh['section'=32,'neuron'=16] {'neuron'}, dimensions={1}, use_global_device_ids=true | all-gather | bytes 417792 | tf_op jit(solution)/shard_map/all_gather | solution.py:46
  47.7 16.8 %all_gather.98 = bf16[6,32768]{1,0:T(8,128)(2,1)S(1)} all-gather(bf16[6,2048]{1,0:T(8,128)(2,1)S(1)} %collective-permute-done.1), channel_id=1, replica_groups=mesh['section'=32,'neuron'=16] {'neuron'}, dimensions={1}, use_global_device_ids=true | all-gather | bytes 417792 | tf_op jit(solution)/shard_map/all_gather | solution.py:46
  69.7 16.3 %all_gather.99 = bf16[6,32768]{1,0:T(8,128)(2,1)S(1)} all-gather(bf16[6,2048]{1,0:T(8,128)(2,1)S(1)} %collective-permute-done.2), channel_id=1, replica_groups=mesh['section'=32,'neuron'=16] {'neuron'}, dimensions={1}, use_global_device_ids=true | all-gather | bytes 417792 | tf_op jit(solution)/shard_map/all_gather | solution.py:46
  91.2 16.8 %all_gather.100 = bf16[6,32768]{1,0:T(8,128)(2,1)S(1)} all-gather(bf16[6,2048]{1,0:T(8,128)(2,1)S(1)} %collective-permute-done.3), channel_id=1, replica_groups=mesh['section'=32,'neuron'=16] {'neuron'}, dimensions={1}, use_global_device_ids=true | all-gather | bytes 417792 | tf_op jit(solution)/shard_map/all_gather | solution.py:46
  113.2 16.4 %all_gather.101 = bf16[6,32768]{1,0:T(8,128)(2,1)S(1)} all-gather(bf16[6,2048]{1,0:T(8,128)(2,1)S(1)} %collective-permute-done.4), channel_id=1, replica_groups=mesh['section'=32,'neuron'=16] {'neuron'}, dimensions={1}, use_global_device_ids=true | all-gather | bytes 417792 | tf_op jit(solution)/shard_map/all_gather | solution.py:46
  134.7 16.8 %all_gather.102 = bf16[6,32768]{1,0:T(8,128)(2,1)S(1)} all-gather(bf16[6,2048]{1,0:T(8,128)(2,1)S(1)} %collective-permute-done.5), channel_id=1, replica_groups=mesh['section'=32,'neuron'=16] {'neuron'}, dimensions={1}, use_global_device_ids=true | all-gather | bytes 417792 | tf_op jit(solution)/shard_map/all_gather | solution.py:46
  156.7 16.4 %all_gather.103 = bf16[6,32768]{1,0:T(8,128)(2,1)S(1)} all-gather(bf16[6,2048]{1,0:T(8,128)(2,1)S(1)} %collective-permute-done.6), channel_id=1, replica_groups=mesh['section'=32,'neuron'=16] {'neuron'}, dimensions={1}, use_global_device_ids=true | all-gather | bytes 417792 | tf_op jit(solution)/shard_map/all_gather | solution.py:46
  178.2 17.2 %all_gather.104 = bf16[6,32768]{1,0:T(8,128)(2,1)S(1)} all-gather(bf16[6,2048]{1,0:T(8,128)(2,1)S(1)} %collective-permute-done.7), channel_id=1, replica_groups=mesh['section'=32,'neuron'=16] {'neuron'}, dimensions={1}, use_global_device_ids=true | all-gather | bytes 417792 | tf_op jit(solution)/shard_map/all_gather | solution.py:46
  200.7 16.4 %all_gather.105 = bf16[6,32768]{1,0:T(8,128)(2,1)S(1)} all-gather(bf16[6,2048]{1,0:T(8,128)(2,1)S(1)} %collective-permute-done.8), channel_id=1, replica_groups=mesh['section'=32,'neuron'=16] {'neuron'}, dimensions={1}, use_global_device_ids=true | all-gather | bytes 417792 | tf_op jit(solution)/shard_map/all_gather | solution.py:46
  222.2 16.8 %all_gather.106 = bf16[6,32768]{1,0:T(8,128)(2,1)S(1)} all-gather(bf16[6,2048]{1,0:T(8,128)(2,1)S(1)} %collective-permute-done.9), channel_id=1, replica_groups=mesh['section'=32,'neuron'=16] {'neuron'}, dimensions={1}, use_global_device_ids=true | all-gather | bytes 417792 | tf_op jit(solution)/shard_map/all_gather | solution.py:46
  244.2 16.4 %all_gather.107 = bf16[6,32768]{1,0:T(8,128)(2,1)S(1)} all-gather(bf16[6,2048]{1,0:T(8,128)(2,1)S(1)} %collective-permute-done.10), channel_id=1, replica_groups=mesh['section'=32,'neuron'=16] {'neuron'}, dimensions={1}, use_global_device_ids=true | all-gather | bytes 417792 | tf_op jit(solution)/shard_map/all_gather | solution.py:46
  265.7 16.8 %all_gather.108 = bf16[6,32768]{1,0:T(8,128)(2,1)S(1)} all-gather(bf16[6,2048]{1,0:T(8,128)(2,1)S(1)} %collective-permute-done.11), channel_id=1, replica_groups=mesh['section'=32,'neuron'=16] {'neuron'}, dimensions={1}, use_global_device_ids=true | all-gather | bytes 417792 | tf_op jit(solution)/shard_map/all_gather | solution.py:46
  287.6 16.4 %all_gather.109 = bf16[6,32768]{1,0:T(8,128)(2,1)S(1)} all-gather(bf16[6,2048]{1,0:T(8,128)(2,1)S(1)} %collective-permute-done.12), channel_id=1, replica_groups=mesh['section'=32,'neuron'=16] {'neuron'}, dimensions={1}, use_global_device_ids=true | all-gather | bytes 417792 | tf_op jit(solution)/shard_map/all_gather | solution.py:46
  309.2 16.7 %all_gather.110 = bf16[6,32768]{1,0:T(8,128)(2,1)S(1)} all-gather(bf16[6,2048]{1,0:T(8,128)(2,1)S(1)} %collective-permute-done.13), channel_id=1, replica_groups=mesh['section'=32,'neuron'=16] {'neuron'}, dimensions={1}, use_global_device_ids=true | all-gather | bytes 417792 | tf_op jit(solution)/shard_map/all_gather | solution.py:46
  331.2 16.4 %all_gather.111 = bf16[6,32768]{1,0:T(8,128)(2,1)S(1)} all-gather(bf16[6,2048]{1,0:T(8,128)(2,1)S(1)} %collective-permute-done.14), channel_id=1, replica_groups=mesh['section'=32,'neuron'=16] {'neuron'}, dimensions={1}, use_global_device_ids=true | all-gather | bytes 417792 | tf_op jit(solution)/shard_map/all_gather | solution.py:46
  352.6 16.9 %all_gather.112 = bf16[6,32768]{1,0:T(8,128)(2,1)S(1)} all-gather(bf16[6,2048]{1,0:T(8,128)(2,1)S(1)} %collective-permute-done.15), channel_id=1, replica_groups=mesh['section'=32,'neuron'=16] {'neuron'}, dimensions={1}, use_global_device_ids=true | all-gather | bytes 417792 | tf_op jit(solution)/shard_map/all_gather | solution.py:46
  374.6 16.4 %all_gather.113 = bf16[6,32768]{1,0:T(8,128)(2,1)S(1)} all-gather(bf16[6,2048]{1,0:T(8,128)(2,1)S(1)} %collective-permute-done.16), channel_id=1, replica_groups=mesh['section'=32,'neuron'=16] {'neuron'}, dimensions={1}, use_global_device_ids=true | all-gather | bytes 417792 | tf_op jit(solution)/shard_map/all_gather | solution.py:46
  396.1 16.7 %all_gather.114 = bf16[6,32768]{1,0:T(8,128)(2,1)S(1)} all-gather(bf16[6,2048]{1,0:T(8,128)(2,1)S(1)} %collective-permute-done.17), channel_id=1, replica_groups=mesh['section'=32,'neuron'=16] {'neuron'}, dimensions={1}, use_global_device_ids=true | all-gather | bytes 417792 | tf_op jit(solution)/shard_map/all_gather | solution.py:46
  417.9 16.4 %all_gather.115 = bf16[6,32768]{1,0:T(8,128)(2,1)S(1)} all-gather(bf16[6,2048]{1,0:T(8,128)(2,1)S(1)} %collective-permute-done.18), channel_id=1, replica_groups=mesh['section'=32,'neuron'=16] {'neuron'}, dimensions={1}, use_global_device_ids=true | all-gather | bytes 417792 | tf_op jit(solution)/shard_map/all_gather | solution.py:46
  439.3 16.7 %all_gather.116 = bf16[6,32768]{1,0:T(8,128)(2,1)S(1)} all-gather(bf16[6,2048]{1,0:T(8,128)(2,1)S(1)} %collective-permute-done.19), channel_id=1, replica_groups=mesh['section'=32,'neuron'=16] {'neuron'}, dimensions={1}, use_global_device_ids=true | all-gather | bytes 417792 | tf_op jit(solution)/shard_map/all_gather | solution.py:46
  461.1 16.4 %all_gather.117 = bf16[6,32768]{1,0:T(8,128)(2,1)S(1)} all-gather(bf16[6,2048]{1,0:T(8,128)(2,1)S(1)} %collective-permute-done.20), channel_id=1, replica_groups=mesh['section'=32,'neuron'=16] {'neuron'}, dimensions={1}, use_global_device_ids=true | all-gather | bytes 417792 | tf_op jit(solution)/shard_map/all_gather | solution.py:46
  482.6 16.7 %all_gather.118 = bf16[6,32768]{1,0:T(8,128)(2,1)S(1)} all-gather(bf16[6,2048]{1,0:T(8,128)(2,1)S(1)} %collective-permute-done.21), channel_id=1, replica_groups=mesh['section'=32,'neuron'=16] {'neuron'}, dimensions={1}, use_global_device_ids=true | all-gather | bytes 417792 | tf_op jit(solution)/shard_map/all_gather | solution.py:46
  504.4 16.4 %all_gather.119 = bf16[6,32768]{1,0:T(8,128)(2,1)S(1)} all-gather(bf16[6,2048]{1,0:T(8,128)(2,1)S(1)} %collective-permute-done.22), channel_id=1, replica_groups=mesh['section'=32,'neuron'=16] {'neuron'}, dimensions={1}, use_global_device_ids=true | all-gather | bytes 417792 | tf_op jit(solution)/shard_map/all_gather | solution.py:46
  525.9 16.9 %all_gather.120 = bf16[6,32768]{1,0:T(8,128)(2,1)S(1)} all-gather(bf16[6,2048]{1,0:T(8,128)(2,1)S(1)} %collective-permute-done.23), channel_id=1, replica_groups=mesh['section'=32,'neuron'=16] {'neuron'}, dimensions={1}, use_global_device_ids=true | all-gather | bytes 417792 | tf_op jit(solution)/shard_map/all_gather | solution.py:46
  547.8 16.4 %all_gather.121 = bf16[6,32768]{1,0:T(8,128)(2,1)S(1)} all-gather(bf16[6,2048]{1,0:T(8,128)(2,1)S(1)} %collective-permute-done.24), channel_id=1, replica_groups=mesh['section'=32,'neuron'=16] {'neuron'}, dimensions={1}, use_global_device_ids=true | all-gather | bytes 417792 | tf_op jit(solution)/shard_map/all_gather | solution.py:46
  569.3 16.7 %all_gather.122 = bf16[6,32768]{1,0:T(8,128)(2,1)S(1)} all-gather(bf16[6,2048]{1,0:T(8,128)(2,1)S(1)} %collective-permute-done.25), channel_id=1, replica_groups=mesh['section'=32,'neuron'=16] {'neuron'}, dimensions={1}, use_global_device_ids=true | all-gather | bytes 417792 | tf_op jit(solution)/shard_map/all_gather | solution.py:46
  591.1 16.4 %all_gather.123 = bf16[6,32768]{1,0:T(8,128)(2,1)S(1)} all-gather(bf16[6,2048]{1,0:T(8,128)(2,1)S(1)} %collective-permute-done.26), channel_id=1, replica_groups=mesh['section'=32,'neuron'=16] {'neuron'}, dimensions={1}, use_global_device_ids=true | all-gather | bytes 417792 | tf_op jit(solution)/shard_map/all_gather | solution.py:46
  612.6 16.7 %all_gather.124 = bf16[6,32768]{1,0:T(8,128)(2,1)S(1)} all-gather(bf16[6,2048]{1,0:T(8,128)(2,1)S(1)} %collective-permute-done.27), channel_id=1, replica_groups=mesh['section'=32,'neuron'=16] {'neuron'}, dimensions={1}, use_global_device_ids=true | all-gather | bytes 417792 | tf_op jit(solution)/shard_map/all_gather | solution.py:46
  634.3 16.5 %all_gather.125 = bf16[6,32768]{1,0:T(8,128)(2,1)S(1)} all-gather(bf16[6,2048]{1,0:T(8,128)(2,1)S(1)} %collective-permute-done.28), channel_id=1, replica_groups=mesh['section'=32,'neuron'=16] {'neuron'}, dimensions={1}, use_global_device_ids=true | all-gather | bytes 417792 | tf_op jit(solution)/shard_map/all_gather | solution.py:46
  655.9 16.7 %all_gather.126 = bf16[6,32768]{1,0:T(8,128)(2,1)S(1)} all-gather(bf16[6,2048]{1,0:T(8,128)(2,1)S(1)} %collective-permute-done.29), channel_id=1, replica_groups=mesh['section'=32,'neuron'=16] {'neuron'}, dimensions={1}, use_global_device_ids=true | all-gather | bytes 417792 | tf_op jit(solution)/shard_map/all_gather | solution.py:46
  679.2 107.5 %collective-permute-done.30 = bf16[6,2048]{1,0:T(8,128)(2,1)S(1)} collective-permute-done((bf16[6,2048]{1,0:T(8,128)(2,1)S(1)}, bf16[6,2048]{1,0:T(8,128)(2,1)S(1)}, u32[]{:S(2)}, u32[]{:S(2)}) %collective-permute-start.30) | collective-permute-done | bytes 24608 | tf_op jit(solution)/shard_map/ppermute | solution.py:52
  786.7 17.9 %all_gather.127 = bf16[6,32768]{1,0:T(8,128)(2,1)S(1)} all-gather(bf16[6,2048]{1,0:T(8,128)(2,1)S(1)} %collective-permute-done.30), channel_id=1, replica_groups=mesh['section'=32,'neuron'=16] {'neuron'}, dimensions={1}, use_global_device_ids=true | all-gather | bytes 417792 | tf_op jit(solution)/shard_map/all_gather | solution.py:46
  (216 shorter events, 181.4 us)
Async XLA Ops:
  0.7 41.9 %copy-start.1 = (s32[1024]{0:T(1024)}, s32[1024]{0:T(1024)S(1)}, u32[]{:S(2)}) copy-start(s32[1024]{0:T(1024)S(1)} %pad_clamp_fusion) | copy-start | bytes 12292
  25.5 0.7 collective-permute-start
  47.0 0.7 collective-permute-start.1
  69.0 0.7 collective-permute-start.2
  90.5 0.7 collective-permute-start.3
  112.5 0.7 collective-permute-start.4
  134.1 0.7 collective-permute-start.5
  156.0 0.7 collective-permute-start.6
  177.6 0.7 collective-permute-start.7
  200.0 0.7 collective-permute-start.8
  221.5 0.7 collective-permute-start.9
  243.5 0.7 collective-permute-start.10
  265.0 0.7 collective-permute-start.11
  287.0 0.7 collective-permute-start.12
  308.5 0.7 collective-permute-start.13
  330.5 0.7 collective-permute-start.14
  352.0 0.7 collective-permute-start.15
  373.9 0.7 collective-permute-start.16
  395.4 0.7 collective-permute-start.17
  417.2 0.7 collective-permute-start.18
  438.7 0.7 collective-permute-start.19
  460.4 0.7 collective-permute-start.20
  481.9 0.7 collective-permute-start.21
  503.7 0.7 collective-permute-start.22
  525.2 0.7 collective-permute-start.23
  547.2 0.7 collective-permute-start.24
  568.7 0.7 collective-permute-start.25
  590.4 0.7 collective-permute-start.26
  611.9 0.7 collective-permute-start.27
  633.7 0.7 collective-permute-start.28
  655.2 0.7 collective-permute-start.29
  676.9 109.8 %collective-permute-start.30 = (bf16[6,2048]{1,0:T(8,128)(2,1)S(1)}, bf16[6,2048]{1,0:T(8,128)(2,1)S(1)}, u32[]{:S(2)}, u32[]{:S(2)}) collective-permute-start(bf16[6,2048]{1,0:T(8,128)(2,1)S(1)} %bitcast.647), channel_id=1, source_target_pairs={{480,496},{481,497},{482,498},{483,499},{484,500},{485,501},{486,5... | collective-permute-start | bytes 73736 | tf_op jit(solution)/shard_map/ppermute | solution.py:52
  (2 other events, 64.6 us)
where the time goes:
time: 820 us; the launch traced here: 810 us
  blocking collectives  536 us (65%)
  matrix products  117 us (14%)
  waiting for transfers between devices  108 us (13%)
  local copies, waits for them, and re-layouts  25.1 us (3%)
  starting transfers between devices  21.2 us (3%)
    all_gather x32, blocking collectives, step(): gathered = lax.all_gather(current, 'neuron', axis=1, tiled=True)  536 us
    dot_general x32, matrix products, layer_apply(): jnp.einsum('msk,skj->msj', picked, weight_tiles[0], preferred_element_typ...  108 us
    ppermute x31, waiting for transfers between devices, step(): return (lax.ppermute(result, 'section', route), collected)  108 us
    gather x32, local copies, waits for them, and re-layouts, layer_apply(): picked = shaped.at[:, source].get(mode='promise_in_bounds')  23.9 us
    ppermute x31, starting transfers between devices, step(): return (lax.ppermute(result, 'section', route), collected)  21.2 us
  transfers between devices with their start and end apart: 31, of which 1 were waited for; matrix products, arithmetic and copies ran while one was open for 0% of the time, Pallas kernels for 0%

commit v1 on v0

--- a/solution.py
+++ b/solution.py
@@ -6,6 +6,32 @@
 NEURON_BIAS = -0.3
 CLIP_LEVEL = 32.0
 UNROLL = True
+
+
+def panels_save(v0, at_axis):
+    local_part = list(v0.shape[1:])
+    local_part[at_axis] *= v0.shape[0]
+    g_now = jnp.moveaxis(v0, 0, at_axis).reshape(local_part)
+    return g_now
+
+
+def create_the_arrays(work_x, ax_name, row_dim):
+    cores_n = lax.psum(1, ax_name)
+    copies = tuple(((rr, (rr + 1) % cores_n) for rr in range(cores_n)))
+    gallery = tuple(((u, idx) for idx, u in copies))
+    state_now, block_next = ([], [])
+    for dev in range(cores_n - 1):
+        if dev % 2 == 0:
+            state_now.append(lax.ppermute(state_now[-1] if state_now else work_x, ax_name, copies))
+        else:
+            block_next.append(
+                lax.ppermute(block_next[-1] if block_next else work_x, ax_name, gallery)
+            )
+    x_new = jnp.stack([*state_now[::-1], work_x, *block_next])
+    right_arr = lax.axis_index(ax_name) - len(state_now)
+    x_new = x_new[(jnp.arange(cores_n) - right_arr) % cores_n]
+    plain = panels_save(x_new, row_dim)
+    return plain
 
 
 def layer_apply(gathered, weight_tiles, source, selector):
@@ -43,7 +69,7 @@
         return jnp.zeros((row_count, shard_width), jnp.bfloat16)
 
     def step(step_num, current, collected, route):
-        gathered = lax.all_gather(current, "neuron", axis=1, tiled=True)
+        gathered = create_the_arrays(current, "neuron", 1)
         active = section_pos == step_num
         result = compute(gathered)
         collected = jnp.where(active, result, collected)

time: 820 us -> 1800 us (2.20)
  the two profiles are of different devices: /device:TPU:455 before, /device:TPU:511 now
where the time goes in v1:
time: 1800 us; the launch traced here: 1790 us
  starting transfers between devices  916 us (51%)
  waiting for transfers between devices  382 us (21%)
  local copies, waits for them, and re-layouts  366 us (20%)
  matrix products  117 us (6%)
    ppermute x256, starting transfers between devices, create_the_arrays(): lax.ppermute(state_now[-1] if state_now else work_x, ax_name, copies)  893 us
    unnamed x517, local copies, waits for them, and re-layouts  268 us
    ppermute x256, waiting for transfers between devices, create_the_arrays(): lax.ppermute(state_now[-1] if state_now else work_x, ax_name, copies)  257 us
    ppermute x31, waiting for transfers between devices, step(): return (lax.ppermute(result, 'section', route), collected)  111 us
    dot_general x32, matrix products, layer_apply(): jnp.einsum('msk,skj->msj', picked, weight_tiles[0], preferred_element_typ...  108 us
    gather x32, local copies, waits for them, and re-layouts, create_the_arrays(): x_new = x_new[(jnp.arange(cores_n) - right_arr) % cores_n]  52.5 us
  transfers between devices with their start and end apart: 511, of which 264 were waited for; matrix products, arithmetic and copies ran while one was open for 15% of the time, Pallas kernels for 0%

profile of v1, /device:TPU:511, one launch (start us, length us, event | category | flops | bytes accessed | tf_op | source)
XLA Modules:
  0.0 1785.1 jit_solution(14044597562548292330)
XLA Ops:
  5.8 3.5 collective-permute-start.2
  92.9 3.5 collective-permute-start.32
  146.1 3.5 collective-permute-start.48
  199.3 3.5 collective-permute-start.64
  252.5 3.5 collective-permute-start.80
  305.8 3.5 collective-permute-start.96
  359.0 3.5 collective-permute-start.112
  412.2 3.5 collective-permute-start.128
  465.4 3.5 collective-permute-start.144
  518.6 3.5 collective-permute-start.160
  571.8 3.5 collective-permute-start.176
  625.0 3.5 collective-permute-start.192
  678.4 3.5 collective-permute-start.208
  731.6 3.5 collective-permute-start.224
  784.8 3.5 collective-permute-start.240
  880.4 3.5 collective-permute-start.272
  933.6 3.5 collective-permute-start.288
  987.2 3.5 collective-permute-start.304
  1040.4 3.5 collective-permute-start.320
  1093.6 3.5 collective-permute-start.336
  1146.8 3.5 collective-permute-start.352
  1200.0 3.5 collective-permute-start.368
  1253.2 3.5 collective-permute-start.384
  1306.4 3.5 collective-permute-start.400
  1359.7 3.5 collective-permute-start.416
  1412.9 3.5 collective-permute-start.432
  1466.1 3.5 collective-permute-start.448
  1519.3 3.5 collective-permute-start.464
  1572.5 3.5 collective-permute-start.480
  1626.3 111.2 %collective-permute-done.495 = bf16[6,2048]{1,0:T(8,128)(2,1)S(1)} collective-permute-done((bf16[6,2048]{1,0:T(8,128)(2,1)S(1)}, bf16[6,2048]{1,0:T(8,128)(2,1)S(1)}, u32[]{:S(2)}, u32[]{:S(2)}) %collective-permute-start.495) | collective-permute-done | bytes 24608 | tf_op jit(solution)/shard_map/ppermute | solution.py:78
  1737.5 4.1 collective-permute-start.496
  1774.7 4.3 collective-permute-done.510
  (1690 shorter events, 1559.9 us)
Async XLA Ops:
  75.1 10.2 collective-permute-start.30
  128.3 10.2 collective-permute-start.46
  181.5 10.2 collective-permute-start.62
  234.7 10.2 collective-permute-start.78
  287.9 10.2 collective-permute-start.94
  341.2 10.2 collective-permute-start.110
  394.4 10.2 collective-permute-start.126
  447.6 10.2 collective-permute-start.142
  500.8 10.2 collective-permute-start.158
  554.0 10.2 collective-permute-start.174
  607.2 10.2 collective-permute-start.190
  660.4 10.2 collective-permute-start.206
  713.8 10.2 collective-permute-start.222
  767.0 10.2 collective-permute-start.238
  862.7 10.2 collective-permute-start.270
  915.8 10.2 collective-permute-start.286
  969.0 10.2 collective-permute-start.302
  1022.6 10.2 collective-permute-start.318
  1075.8 10.2 collective-permute-start.334
  1129.0 10.2 collective-permute-start.350
  1182.2 10.2 collective-permute-start.366
  1235.4 10.2 collective-permute-start.382
  1288.6 10.2 collective-permute-start.398
  1341.8 10.2 collective-permute-start.414
  1395.1 10.2 collective-permute-start.430
  1448.3 10.2 collective-permute-start.446
  1501.5 10.2 collective-permute-start.462
  1554.7 10.2 collective-permute-start.478
  1607.9 10.2 collective-permute-start.494
  1625.0 112.5 %collective-permute-start.495 = (bf16[6,2048]{1,0:T(8,128)(2,1)S(1)}, bf16[6,2048]{1,0:T(8,128)(2,1)S(1)}, u32[]{:S(2)}, u32[]{:S(2)}) collective-permute-start(bf16[6,2048]{1,0:T(8,128)(2,1)S(1)} %bitcast.1797), channel_id=1, source_target_pairs={{480,496},{481,497},{482,498},{483,499},{484,500},{485,501},{486,5... | collective-permute-start | bytes 73736 | tf_op jit(solution)/shard_map/ppermute | solution.py:78
  1737.5 5.1 collective-permute-start.496
  1768.9 5.5 collective-permute-start.509
  (482 other events, 2207.8 us)
